TPU v7x, 128 devices: a whole 4x4x4 slice. The times are simulated.
128 devices in a mesh: segment: 8 (over x, core), blk: 16 (over y, z).
Axes of the slice: x: 4, y: 4, z: 4, core: 2. Of those that a mesh axis runs over, the one named last changes fastest.
Arguments:
- fresh: bfloat16 [256, 4096], replicated, may hold values from -6 to 6
- previous: bfloat16 [8, 256, 4096], P('segment'), may hold values from -6 to 6
- span_index: int32 [8], P('segment'), may hold values from 0 to 7
- cache_counts: int32 [8, 16], P('segment'), may hold values from 1 to 2048, 16384 in all within a row
- norm_gain: float32 [8, 4096], P('segment'), may hold values from 0.1 to 1.9
- w_query: bfloat16 [8, 4096, 4096], P('segment', None, 'blk'), may hold values from -0.375 to 0.375
- w_keyval: bfloat16 [8, 4096, 2048], P('segment', None, 'blk'), may hold values from -0.09375 to 0.09375
- w_out: bfloat16 [8, 4096, 4096], P('segment', 'blk'), may hold values from -0.09375 to 0.09375
- cache_keys: bfloat16 [8, 32768, 1024], P('segment', 'blk'), may hold values from -220 to 220
- cache_values: bfloat16 [8, 32768, 1024], P('segment', 'blk'), may hold values from -6 to 6
Outputs:
- mixed: bfloat16 [8, 256, 4096], P('segment')
Inputs may be any that keep to these rules, and one draw needn't show every extreme that they name: Each row of cache_counts sums to 16384 and its largest entry is 2048.
All inputs are finite; a program needn't handle non-finite values.
Results may differ from a plain program's by a relative error of at most 0.012.
Values may be sent and summed in bfloat16 or wider, within the bound.
No kernel may reach another device: no remote copies, remote signals or barrier semaphores. Data moves between devices by JAX's collectives and lax.ppermute only.
A program may use at most 128 MiB of HBM per device.

v0:
```python
import jax
import jax.numpy as jnp
from jax import lax
from jax.sharding import PartitionSpec as P

KVH = 8
HD = 128
ROPE_BASE = 500000.0
EPSILON = 1e-05


def passed_along(block, axis, distance):
    devices = range(lax.axis_size(axis))
    route = [(i - distance, i) for i in devices if i - distance in devices]
    return lax.ppermute(block, axis, route)


def swapped(block, axis, distance):
    count = lax.axis_size(axis)
    route = []
    for low in range(count):
        high = low | 1 << distance
        if high != low and high < count:
            route += [(low, high), (high, low)]
    return lax.ppermute(block, axis, route)


def rotate(projected, first_span):
    length = projected.shape[0]
    half_width = projected.shape[-1] // 2
    positions = (first_span * length + jnp.arange(length, dtype=jnp.int32)).astype(jnp.float32)
    inverse = ROPE_BASE ** (
        -(jnp.arange(half_width, dtype=jnp.float32) * 2.0) / projected.shape[-1]
    )
    angles = positions[:, None] * inverse[None, :]
    cosine = jnp.cos(angles)[:, None, :]
    sine_table = jnp.sin(angles)[:, None, :]
    left_part = projected[..., :half_width]
    right_part = projected[..., half_width:]
    return jnp.concatenate(
        [
            left_part * cosine - right_part * sine_table,
            right_part * cosine + left_part * sine_table,
        ],
        axis=-1,
    )


def attend_rows(query_rows, key_rows, value_rows, allowed):
    scores = lax.dot_general(
        query_rows, key_rows, (((1,), (1,)), ((), ())), preferred_element_type=jnp.float32
    ) * query_rows.shape[-1] ** (-0.5)
    scores = jnp.where(allowed, scores, -jnp.inf)
    highest = jnp.max(scores, axis=-1, keepdims=True)
    weights = jnp.exp(scores - highest)
    totals = jnp.sum(weights, axis=-1, keepdims=True)
    partial_out = (
        jnp.dot(weights.astype(jnp.bfloat16), value_rows, preferred_element_type=jnp.float32)
        / totals
    ).astype(jnp.bfloat16)
    return (partial_out, (highest + jnp.log(totals))[:, 0])


def shards(
    fresh,
    previous,
    span_index,
    cache_counts,
    norm_gain,
    w_query,
    w_keyval,
    w_out,
    cache_keys,
    cache_values,
):
    blocks = lax.axis_size("blk")
    position = lax.axis_index("blk")
    span_rows = fresh.shape[0]
    arrived = passed_along(previous[0], "segment", 1)
    current = jnp.where(lax.axis_index("segment") == 0, fresh, arrived)
    widened = current.astype(jnp.float32)
    normed = (
        widened
        * lax.rsqrt(jnp.mean(widened * widened, axis=-1, keepdims=True) + EPSILON)
        * norm_gain[0]
    ).astype(jnp.bfloat16)
    first_span = span_index[0]
    heads_here = w_query.shape[2] // HD
    ratio = blocks // KVH
    queries = jnp.dot(normed, w_query[0], preferred_element_type=jnp.float32).reshape(
        span_rows, heads_here, HD
    )
    queries = rotate(queries, first_span).astype(jnp.bfloat16).reshape(span_rows, heads_here * HD)
    projected = jnp.dot(normed, w_keyval[0], preferred_element_type=jnp.float32)
    odd_member = position % 2 == 1
    as_key = rotate(projected[:, None, :], first_span)[:, 0, :].astype(jnp.bfloat16)
    mine = jnp.where(odd_member, projected.astype(jnp.bfloat16), as_key)
    partner = swapped(mine, "blk", 0)
    own_keys = jnp.where(odd_member, partner, mine)
    own_values = jnp.where(odd_member, mine, partner)
    query_rows = queries.reshape(span_rows * heads_here, HD)
    row_tokens = jnp.arange(span_rows * heads_here, dtype=jnp.int32) // heads_here
    causal = row_tokens[:, None] >= jnp.arange(span_rows, dtype=jnp.int32)[None, :]
    own_out, own_log = attend_rows(query_rows, own_keys, own_values, causal)
    own_out = own_out.reshape(span_rows, heads_here * HD)
    own_log = own_log.reshape(span_rows, heads_here).T
    cache_rows = cache_keys.shape[1]
    offsets = jnp.arange(cache_rows, dtype=jnp.int32)
    every_query = lax.all_gather(queries, "blk", axis=0, tiled=True)
    live = cache_counts[0, position]

    def holder(source):
        query_block = lax.dynamic_slice_in_dim(
            every_query, source * span_rows, span_rows, 0
        ).reshape(span_rows * heads_here, HD)
        head_start = source // ratio * HD
        key_rows = lax.dynamic_slice_in_dim(cache_keys[0], head_start, HD, 1)
        value_rows = lax.dynamic_slice_in_dim(cache_values[0], head_start, HD, 1)
        partial_out, log_totals = attend_rows(
            query_block, key_rows, value_rows, (offsets < live)[None, :]
        )
        return (
            partial_out.reshape(span_rows, heads_here * HD),
            log_totals.reshape(span_rows, heads_here).T,
        )

    held_outs, held_logs = lax.map(holder, jnp.arange(blocks, dtype=jnp.int32))
    shard_outs = lax.all_to_all(held_outs, "blk", split_axis=0, concat_axis=0, tiled=True)
    shard_logs = lax.all_to_all(held_logs, "blk", split_axis=0, concat_axis=0, tiled=True)
    all_outs = (
        jnp.concatenate([own_out[None], shard_outs], axis=0)
        .astype(jnp.float32)
        .reshape(blocks + 1, span_rows, heads_here, HD)
    )
    all_logs = jnp.concatenate([own_log[None], shard_logs], axis=0).transpose(0, 2, 1)
    ceiling = jnp.max(all_logs, axis=0)
    factors = jnp.exp(all_logs - ceiling)
    attended = (
        jnp.sum(factors[..., None] * all_outs, axis=0) / jnp.sum(factors, axis=0)[..., None]
    ).astype(jnp.bfloat16)
    attended = attended.reshape(span_rows, heads_here * HD)
    head_terms = lax.optimization_barrier(
        jnp.dot(attended, w_out[0], preferred_element_type=jnp.float32).astype(jnp.bfloat16)
    ).astype(jnp.float32)
    summed = lax.psum(head_terms.astype(jnp.bfloat16), "blk").astype(jnp.float32)
    mixed = (widened + summed).astype(jnp.bfloat16)
    return mixed[None]


def solution(mesh):
    placed = (
        P(),
        P("segment", None, None),
        P("segment"),
        P("segment", None),
        P("segment", None),
        P("segment", None, "blk"),
        P("segment", None, "blk"),
        P("segment", "blk", None),
        P("segment", "blk", None),
        P("segment", "blk", None),
    )
    return jax.shard_map(
        shards, mesh=mesh, in_specs=placed, out_specs=P("segment", None, None), check_vma=False
    )
```

profile of v0, /device:TPU:0, one launch (start us, length us, event | category | flops | bytes accessed | tf_op | source)
XLA Modules:
  0.0 425.8 jit_solution(5192613194957220926)
XLA Ops:
  6.5 2.8 collective-permute-start
  9.3 4.1 copy.33
  14.4 2.7 fusion.23
  19.9 67.0 %all-gather.2.cloned.1.call-done = bf16[4096,256]{1,0:T(8,128)(2,1)} async-done(((bf16[256,256]{1,0:T(8,128)(2,1)}), bf16[4096,256]{1,0:T(8,128)(2,1)}) %all-gather.2.cloned.1.call-update) | async-done | bytes 2097168 | tf_op jit(solution)/shard_map/all_gather | solution.py:109
  87.0 177.8 %while.15 = (s32[]{:T(128)}, bf16[16,256,256]{2,1,0:T(8,128)(2,1)}, f32[16,2,256]{2,1,0:T(2,128)S(1)}, s32[]{:T(128)}, s32[16]{0:T(128)S(1)}, /*index=5*/bf16[40...) while((s32[]{:T(128)}, bf16[16,256,256]{2,1,0:T(8,128)(2,1)}, ...), condition=%wide.region_6.7_spmd.clone, body=%wide.region_3.6_spmd.clone.sunk | while | flops 548537856 | bytes 14979499 | solution.py:127
  92.3 1.9 fusion.77
  95.1 2.0 fusion.79
  103.4 1.9 fusion.77
  106.2 2.0 fusion.79
  114.5 1.9 fusion.77
  117.3 2.0 fusion.79
  125.6 1.9 fusion.77
  128.4 2.0 fusion.79
  136.7 1.9 fusion.77
  139.5 2.0 fusion.79
  147.8 1.9 fusion.77
  150.6 2.0 fusion.79
  159.0 1.9 fusion.77
  161.8 2.0 fusion.79
  170.1 1.9 fusion.77
  172.9 2.0 fusion.79
  181.2 1.9 fusion.77
  184.0 2.0 fusion.79
  192.3 1.9 fusion.77
  195.1 2.0 fusion.79
  203.4 1.9 fusion.77
  206.2 2.0 fusion.79
  214.5 1.9 fusion.77
  217.3 2.0 fusion.79
  225.6 1.9 fusion.77
  228.5 2.0 fusion.79
  236.8 1.9 fusion.77
  239.6 2.0 fusion.79
  247.9 1.9 fusion.77
  250.7 2.0 fusion.79
  259.0 1.9 fusion.77
  261.8 2.0 fusion.79
  264.8 12.4 %all_to_all.10 = f32[16,2,256]{2,1,0:T(2,128)S(1)} all-to-all(f32[16,2,256]{2,1,0:T(2,128)S(1)} %get-tuple-element.120), channel_id=1, replica_groups=mesh['segment'=8,'blk'=16] {'blk'}, dimensions={0} | all-to-all | bytes 65536 | tf_op jit(solution)/shard_map/all_to_all | solution.py:129
  277.2 4.4 %all-to-all-start.1 = ((bf16[16,256,256]{2,1,0:T(8,128)(2,1)}), bf16[16,256,256]{2,1,0:T(8,128)(2,1)}, u32[]{:S(2)}, u32[]{:S(2)}) async-start(bf16[16,256,256]{2,1,0:T(8,128)(2,1)} %get-tuple-element.121), calls=%async_computation.1 | async-start | bytes 4194304 | tf_op jit(solution)/shard_map/all_to_all | solution.py:128
  281.6 2.8 fusion.33
  284.8 1.8 collective-permute-start.1
  286.9 18.0 %collective-permute-done.1 = bf16[256,128]{0,1:T(8,128)(2,1)S(1)} collective-permute-done((bf16[256,128]{0,1:T(8,128)(2,1)S(1)}, bf16[256,128]{0,1:T(8,128)(2,1)S(1)}, u32[]{:S(2)}, u32[]{:S(2)}) %collective-permute-start.1) | collective-permute-done | bytes 65568 | tf_op jit(solution)/shard_map/ppermute | solution.py:25
  306.0 2.1 copy.31
  309.4 4.0 concatenate.34
  313.4 7.7 %multiply_reduce_fusion = f32[256,2,128]{2,1,0:T(2,128)S(1)} fusion(bf16[16,256,2,128]{3,2,1,0:T(2,128)(2,1)} %concatenate.34, bf16[1,256,2,128]{3,2,1,0:T(2,128)(2,1)S(1)} %bitcast.73, f32[17,256,2]{2,1,0:T(8,128)} %copy.31), kind=kLoop, calls=%fused_computation.28 | loop fusion | flops 4390912 | bytes 2525184 | tf_op jit(solution)/shard_map/reduce_sum | solution.py:139
  321.5 2.0 convolution_convert_fusion
  323.5 91.1 %all-reduce.2.cloned.1.call-done = bf16[256,4096]{1,0:T(8,128)(2,1)} async-done(((bf16[256,4096]{1,0:T(8,128)(2,1)}), bf16[256,4096]{1,0:T(8,128)(2,1)}) %all-reduce.2.cloned.1.call-update) | async-done | bytes 2097168 | tf_op jit(solution)/shard_map/psum | solution.py:145
  414.6 4.3 %fusion.27 = bf16[1,256,4096]{2,1,0:T(8,128)(2,1)} fusion(bf16[256,4096]{1,0:T(8,128)(2,1)} %all-reduce.2.cloned.1.call-done, bf16[256,4096]{1,0:T(8,128)(2,1)} %copy-done.1), kind=kLoop, calls=%fused_computation.33 | loop fusion | flops 4194304 | bytes 6291456 | tf_op jit(solution)/shard_map/broadcast_in_dim | solution.py:147
  (219 shorter events, 71.7 us)
Async XLA Ops:
  6.5 314.9 %copy-start = (bf16[1,256,4096]{2,1,0:T(8,128)(2,1)S(1)}, bf16[1,256,4096]{2,1,0:T(8,128)(2,1)}, u32[]{:S(2)}) copy-start(bf16[1,256,4096]{2,1,0:T(8,128)(2,1)} %param.19) | copy-start | bytes 6291460
  6.5 80.4 %all-gather.2.cloned.1.call-start = ((), (), s32[]{:S(2)}) async-start(), calls=%async_computation.2 | async-start | bytes 2228224 | tf_op jit(solution)/shard_map/all_gather | solution.py:109
  6.5 7.9 %collective-permute-start = (bf16[256,4096]{1,0:T(8,128)(2,1)}, bf16[256,4096]{1,0:T(8,128)(2,1)}, u32[]{:S(2)}, u32[]{:S(2)}) collective-permute-start(bf16[256,4096]{1,0:T(8,128)(2,1)} %bitcast.76), channel_id=1, source_target_pairs={{0,16},{16,32},{32,48},{48,64},{64,80},{80,96},{96,112},{1,17},{17... | collective-permute-start | bytes 6291464 | tf_op jit(solution)/shard_map/ppermute | solution.py:15
  14.4 2.8 copy-start.2
  14.4 2.8 copy-start.3
  17.1 1.3 copy-start.1
  17.2 2.1 copy-start.4
  277.2 32.3 %all-to-all-start.1 = ((bf16[16,256,256]{2,1,0:T(8,128)(2,1)}), bf16[16,256,256]{2,1,0:T(8,128)(2,1)}, u32[]{:S(2)}, u32[]{:S(2)}) async-start(bf16[16,256,256]{2,1,0:T(8,128)(2,1)} %get-tuple-element.121), calls=%async_computation.1 | async-start | bytes 4194304 | tf_op jit(solution)/shard_map/all_to_all | solution.py:128
  281.6 133.0 %all-reduce.2.cloned.1.call-start = ((), (), s32[]{:S(2)}) async-start(), calls=%async_computation.3 | async-start | bytes 4194304 | tf_op jit(solution)/shard_map/psum | solution.py:145
  284.8 20.1 %collective-permute-start.1 = (bf16[256,128]{0,1:T(8,128)(2,1)S(1)}, bf16[256,128]{0,1:T(8,128)(2,1)S(1)}, u32[]{:S(2)}, u32[]{:S(2)}) collective-permute-start(bf16[256,128]{0,1:T(8,128)(2,1)S(1)} %fusion.54), channel_id=1, source_target_pairs={{0,1},{1,0},{2,3},{3,2},{4,5},{5,4},{6,7},{7,6},{8,9},{9,8},{10,11... | collective-permute-start | bytes 196616 | tf_op jit(solution)/shard_map/ppermute | solution.py:25
Sparse Core Ops, SparseCore 0:
  19.4 67.5 all-gather.1
  323.6 90.9 all-reduce.1
where the time goes:
time: 429 us; the launch traced here: 426 us
  waiting for transfers between devices  177 us (41%)
  matrix products  68.5 us (16%)
  local copies, waits for them, and re-layouts  52.7 us (12%)
  loops' own time  50.4 us (12%)
  other arithmetic  41.1 us (10%)
  between operations  14.3 us (3%)
  blocking collectives  12.4 us (3%)
  starting transfers between devices  9.06 us (2%)
    psum x1, waiting for transfers between devices, shards(): lax.psum(head_terms.astype(jnp.bfloat16), 'blk').astype(jnp.float32)  91.1 us
    all_gather x1, waiting for transfers between devices, shards(): every_query = lax.all_gather(queries, 'blk', axis=0, tiled=True)  67 us
    another operation x1, loops' own time, shards(): held_outs, held_logs = lax.map(holder, jnp.arange(blocks, dtype=jnp.int32))  50.4 us
    dot_general x17, matrix products, attend_rows(): jnp.dot(weights.astype(jnp.bfloat16), value_rows, preferred_element_type=...  32.6 us
    dot_general x17, matrix products, attend_rows(): lax.dot_general(query_rows, key_rows, (((1,), (1,)), ((), ())), preferred...  30.1 us
    ppermute x1, waiting for transfers between devices, swapped(): return lax.ppermute(block, axis, route)  18 us
    reduce_sum x17, other arithmetic, attend_rows(): totals = jnp.sum(weights, axis=-1, keepdims=True)  15.2 us
    dynamic_slice x16, local copies, waits for them, and re-layouts, holder(): lax.dynamic_slice_in_dim(every_query, source * span_rows, span_rows, 0)  14.7 us
  transfers between devices with their start and end apart: 5, of which 4 were waited for; matrix products, arithmetic and copies ran while one was open for 3% of the time, Pallas kernels for 0%

commit v1 on v0

--- a/solution.py
+++ b/solution.py
@@ -142,7 +142,9 @@
     head_terms = lax.optimization_barrier(
         jnp.dot(attended, w_out[0], preferred_element_type=jnp.float32).astype(jnp.bfloat16)
     ).astype(jnp.float32)
-    summed = lax.psum(head_terms.astype(jnp.bfloat16), "blk").astype(jnp.float32)
+    summed = jnp.sum(lax.all_gather(head_terms.astype(jnp.bfloat16), "blk"), axis=0).astype(
+        jnp.float32
+    )
     mixed = (widened + summed).astype(jnp.bfloat16)
     return mixed[None]
 

time: 429 us -> 550 us (1.28)
  waiting for transfers between devices: 177 us -> 284 us
  other arithmetic: 41.1 us -> 55.1 us
    all_gather x0 -> x1, waiting for transfers between devices: none -> 198 us  [shards(): lax.all_gather(head_terms.astype(jnp.bfloat16), 'blk')]
    psum x1 -> x0, waiting for transfers between devices: 91.1 us -> none  [shards(): lax.psum(head_terms.astype(jnp.bfloat16), 'blk').astype(jnp.float32)]
    reduce_sum x0 -> x1, other arithmetic: none -> 13 us  [shards(): jnp.sum(lax.all_gather(head_terms.astype(jnp.bfloat16), 'blk'), axis=0)]
  transfers between devices with their start and end apart: 5 -> 5, of which waited for: 4 -> 4; matrix products, arithmetic and copies ran while one was open for 3% -> 2% of each run, Pallas kernels for 0% -> 0%
where the time goes in v1:
time: 550 us; the launch traced here: 547 us
  waiting for transfers between devices  284 us (52%)
  matrix products  68.4 us (12%)
  other arithmetic  55.1 us (10%)
  local copies, waits for them, and re-layouts  52.6 us (10%)
  loops' own time  50.5 us (9%)
  between operations  14.3 us (3%)
  blocking collectives  12.4 us (2%)
  starting transfers between devices  9.25 us (2%)
    all_gather x1, waiting for transfers between devices, shards(): lax.all_gather(head_terms.astype(jnp.bfloat16), 'blk')  198 us
    all_gather x1, waiting for transfers between devices, shards(): every_query = lax.all_gather(queries, 'blk', axis=0, tiled=True)  67 us
    another operation x1, loops' own time, shards(): held_outs, held_logs = lax.map(holder, jnp.arange(blocks, dtype=jnp.int32))  50.5 us
    dot_general x17, matrix products, attend_rows(): jnp.dot(weights.astype(jnp.bfloat16), value_rows, preferred_element_type=...  32.5 us
    dot_general x17, matrix products, attend_rows(): lax.dot_general(query_rows, key_rows, (((1,), (1,)), ((), ())), preferred...  30.1 us
    ppermute x1, waiting for transfers between devices, swapped(): return lax.ppermute(block, axis, route)  17.8 us
    reduce_sum x17, other arithmetic, attend_rows(): totals = jnp.sum(weights, axis=-1, keepdims=True)  15.2 us
    dynamic_slice x16, local copies, waits for them, and re-layouts, holder(): lax.dynamic_slice_in_dim(every_query, source * span_rows, span_rows, 0)  14.7 us
  transfers between devices with their start and end apart: 5, of which 4 were waited for; matrix products, arithmetic and copies ran while one was open for 2% of the time, Pallas kernels for 0%

profile of v1, /device:TPU:0, one launch (start us, length us, event | category | flops | bytes accessed | tf_op | source)
XLA Modules:
  0.0 546.5 jit_solution(4007755344468016487)
XLA Ops:
  6.5 2.8 collective-permute-start
  10.0 4.1 copy.33
  14.4 2.7 fusion.23
  20.0 67.0 %all-gather.4.cloned.1.call-done = bf16[4096,256]{1,0:T(8,128)(2,1)} async-done(((bf16[256,256]{1,0:T(8,128)(2,1)}), bf16[4096,256]{1,0:T(8,128)(2,1)}) %all-gather.4.cloned.1.call-update) | async-done | bytes 2097168 | tf_op jit(solution)/shard_map/all_gather | solution.py:109
  87.0 178.8 %while.15 = (s32[]{:T(128)}, bf16[16,256,256]{2,1,0:T(8,128)(2,1)}, f32[16,2,256]{2,1,0:T(2,128)S(1)}, s32[]{:T(128)}, s32[16]{0:T(128)S(1)}, /*index=5*/bf16[40...) while((s32[]{:T(128)}, bf16[16,256,256]{2,1,0:T(8,128)(2,1)}, ...), condition=%wide.region_6.7_spmd.clone, body=%wide.region_3.6_spmd.clone.sunk | while | flops 548537856 | bytes 14979499 | solution.py:127
  92.3 1.9 fusion.77
  95.1 2.0 fusion.79
  103.5 1.9 fusion.77
  106.3 2.0 fusion.79
  114.7 1.9 fusion.77
  117.5 2.0 fusion.79
  125.9 1.9 fusion.77
  128.7 2.0 fusion.79
  137.0 1.9 fusion.77
  139.8 2.0 fusion.79
  148.2 1.9 fusion.77
  151.0 2.0 fusion.79
  159.4 1.9 fusion.77
  162.2 2.0 fusion.79
  170.6 1.9 fusion.77
  173.4 2.0 fusion.79
  181.7 1.9 fusion.77
  184.5 2.0 fusion.79
  192.9 1.9 fusion.77
  195.7 2.0 fusion.79
  204.1 1.9 fusion.77
  206.9 2.0 fusion.79
  215.3 1.9 fusion.77
  218.1 2.0 fusion.79
  226.4 1.9 fusion.77
  229.2 2.0 fusion.79
  237.6 1.9 fusion.77
  240.4 2.0 fusion.79
  248.8 1.9 fusion.77
  251.6 2.0 fusion.79
  262.8 2.0 fusion.79
  265.8 12.4 %all_to_all.10 = f32[16,2,256]{2,1,0:T(2,128)S(1)} all-to-all(f32[16,2,256]{2,1,0:T(2,128)S(1)} %get-tuple-element.120), channel_id=1, replica_groups=mesh['segment'=8,'blk'=16] {'blk'}, dimensions={0} | all-to-all | bytes 65536 | tf_op jit(solution)/shard_map/all_to_all | solution.py:129
  278.1 4.4 all-to-all-start.1
  282.6 2.8 fusion.33
  285.8 2.0 collective-permute-start.1
  288.1 17.8 %collective-permute-done.1 = bf16[256,128]{0,1:T(8,128)(2,1)S(1)} collective-permute-done((bf16[256,128]{0,1:T(8,128)(2,1)S(1)}, bf16[256,128]{0,1:T(8,128)(2,1)S(1)}, u32[]{:S(2)}, u32[]{:S(2)}) %collective-permute-start.1) | collective-permute-done | bytes 65568 | tf_op jit(solution)/shard_map/ppermute | solution.py:25
  307.1 2.1 copy.31
  310.4 4.0 concatenate.34
  314.3 7.7 %multiply_reduce_fusion = f32[256,2,128]{2,1,0:T(2,128)S(1)} fusion(bf16[16,256,2,128]{3,2,1,0:T(2,128)(2,1)} %concatenate.34, bf16[1,256,2,128]{3,2,1,0:T(2,128)(2,1)S(1)} %bitcast.75, f32[17,256,2]{2,1,0:T(8,128)} %copy.31), kind=kLoop, calls=%fused_computation.28 | loop fusion | flops 4390912 | bytes 2525184 | tf_op jit(solution)/shard_map/reduce_sum | solution.py:139
  322.4 2.0 convolution_convert_fusion
  324.5 197.9 %all-gather.6.cloned.1.call-done = bf16[4096,4096]{1,0:T(8,128)(2,1)} async-done(((bf16[256,4096]{1,0:T(8,128)(2,1)}), bf16[4096,4096]{1,0:T(8,128)(2,1)}) %all-gather.6.cloned.1.call-update) | async-done | bytes 33554448 | tf_op jit(solution)/shard_map/all_gather | solution.py:145
  522.4 13.0 %reduce_sum.64 = bf16[256,4096]{1,0:T(8,128)(2,1)} reduce(bf16[16,256,4096]{2,1,0:T(8,128)(2,1)} %bitcast.67, bf16[]{:T(256)} %constant.139.clone.1), dimensions={0}, to_apply=%region_10.11 | reduce | flops 15728640 | bytes 35651584 | tf_op jit(solution)/shard_map/reduce_sum | solution.py:145
  535.4 4.3 fusion.27
  (220 shorter events, 74.5 us)
Async XLA Ops:
  6.5 315.9 %copy-start = (bf16[1,256,4096]{2,1,0:T(8,128)(2,1)S(1)}, bf16[1,256,4096]{2,1,0:T(8,128)(2,1)}, u32[]{:S(2)}) copy-start(bf16[1,256,4096]{2,1,0:T(8,128)(2,1)} %param.19) | copy-start | bytes 6291460
  6.5 80.4 %all-gather.4.cloned.1.call-start = ((), (), s32[]{:S(2)}) async-start(), calls=%async_computation.2 | async-start | bytes 2228224 | tf_op jit(solution)/shard_map/all_gather | solution.py:109
  6.5 7.9 %collective-permute-start = (bf16[256,4096]{1,0:T(8,128)(2,1)}, bf16[256,4096]{1,0:T(8,128)(2,1)}, u32[]{:S(2)}, u32[]{:S(2)}) collective-permute-start(bf16[256,4096]{1,0:T(8,128)(2,1)} %bitcast.78), channel_id=1, source_target_pairs={{0,16},{16,32},{32,48},{48,64},{64,80},{80,96},{96,112},{1,17},{17... | collective-permute-start | bytes 6291464 | tf_op jit(solution)/shard_map/ppermute | solution.py:15
  14.4 2.8 copy-start.2
  14.4 2.8 copy-start.3
  17.1 1.3 copy-start.1
  17.2 2.1 copy-start.4
  278.1 32.3 %all-to-all-start.1 = ((bf16[16,256,256]{2,1,0:T(8,128)(2,1)}), bf16[16,256,256]{2,1,0:T(8,128)(2,1)}, u32[]{:S(2)}, u32[]{:S(2)}) async-start(bf16[16,256,256]{2,1,0:T(8,128)(2,1)} %get-tuple-element.121), calls=%async_computation.1 | async-start | bytes 4194304 | tf_op jit(solution)/shard_map/all_to_all | solution.py:128
  282.6 239.8 %all-gather.6.cloned.1.call-start = ((), (), s32[]{:S(2)}) async-start(), calls=%async_computation.3 | async-start | bytes 35651584 | tf_op jit(solution)/shard_map/all_gather | solution.py:145
  285.8 20.1 %collective-permute-start.1 = (bf16[256,128]{0,1:T(8,128)(2,1)S(1)}, bf16[256,128]{0,1:T(8,128)(2,1)S(1)}, u32[]{:S(2)}, u32[]{:S(2)}) collective-permute-start(bf16[256,128]{0,1:T(8,128)(2,1)S(1)} %fusion.54), channel_id=1, source_target_pairs={{0,1},{1,0},{2,3},{3,2},{4,5},{5,4},{6,7},{7,6},{8,9},{9,8},{10,11... | collective-permute-start | bytes 196616 | tf_op jit(solution)/shard_map/ppermute | solution.py:25
Sparse Core Ops, SparseCore 0:
  19.4 67.5 all-gather.3
  324.6 197.7 all-gather.5
